TPU v7x, 256 devices: a whole 4x4x8 slice. The times are simulated.
256 devices in a mesh: neuron: 16 (over z, x_hi), tm: 16 (over y, x_lo, core).
Axes of the slice: x: 4 (x_hi: 2, x_lo: 2; x = x_hi * 2 + x_lo), y: 4, z: 8, core: 2. Of those that a mesh axis runs over, the one named last changes fastest.
Arguments:
- signal: bfloat16 [8192, 65536], P('tm', 'neuron'), may hold values from -6 to 6
- readin: bfloat16 [65536, 256], P('neuron'), may hold values from -0.0234375 to 0.0234375
- proj: bfloat16 [256, 512], replicated, may hold values from -0.375 to 0.375
- kernel: float32 [63, 512], replicated, may hold values from -0.75 to 0.75
- gain: float32 [512], replicated, may hold values from 0.5 to 1.5
- w_one: bfloat16 [512, 2048], P(None, 'neuron'), may hold values from -0.25 to 0.25
- w_two: bfloat16 [2048, 512], P('neuron'), may hold values from -0.125 to 0.125
- cotangent: bfloat16 [8192, 512], P('tm'), may hold values from -6 to 6
Outputs:
- denoised: bfloat16 [8192, 512], P('tm')
- grad_readin: float32 [65536, 256], P(('neuron', 'tm'))
- grad_proj: float32 [256, 512], replicated
- grad_kernel: float32 [63, 512], replicated
- grad_gain: float32 [512], replicated
- grad_w_one: float32 [512, 2048], P(None, 'neuron')
- grad_w_two: float32 [2048, 512], P('neuron')
All inputs are finite; a program needn't handle non-finite values.
Results may differ from a plain program's by a relative error of at most 0.0085.
Values may be sent and summed in bfloat16 or wider, within the bound.
No kernel may reach another device: no remote copies, remote signals or barrier semaphores. Data moves between devices by JAX's collectives and lax.ppermute only.
A program may use at most 64 MiB of HBM per device.

v0:
```python
import jax
import jax.numpy as jnp
from jax import lax
from jax.sharding import PartitionSpec as P


def with_halo(block, sides, width):
    for axis, dim in sides:
        count = lax.axis_size(axis)
        forward = [(i, i + 1) for i in range(count - 1)]
        backward = [(target, source) for source, target in forward]
        low = lax.ppermute(
            lax.slice_in_dim(block, block.shape[dim] - width, None, axis=dim), axis, forward
        )
        high = lax.ppermute(lax.slice_in_dim(block, 0, width, axis=dim), axis, backward)
        block = jnp.concatenate([low, block, high], axis=dim)
    return block


def conv_time(padded, kernel, rows):

    def step(index, total):
        window = lax.dynamic_slice_in_dim(padded, index, rows, 0)
        taps = lax.dynamic_slice_in_dim(kernel, index, 1, 0)
        return total + taps * window

    start = jnp.zeros((rows, padded.shape[1]), jnp.float32)
    return lax.fori_loop(0, kernel.shape[0], step, start)


def over_time(left, right):
    return lax.dot_general(
        left, right, (((0,), (0,)), ((), ())), preferred_element_type=jnp.float32
    )


def body(signal, readin, proj, kernel, gain, w_one, w_two, cotangent):
    rows = signal.shape[0]
    taps = kernel.shape[0]
    half = (taps - 1) // 2
    partial_latent = jnp.dot(signal, readin, preferred_element_type=jnp.float32)
    latent = lax.psum(partial_latent, "neuron").astype(jnp.bfloat16)
    lifted = jnp.dot(latent, proj, preferred_element_type=jnp.float32)
    padded = with_halo(lifted, (("tm", 0),), half)
    mixed = lifted + conv_time(padded, kernel, rows)
    scale = lax.rsqrt(jnp.mean(mixed * mixed, axis=1, keepdims=True) + 1e-05)
    normed = (mixed * scale * gain[None, :]).astype(jnp.bfloat16)
    pre = jnp.dot(normed, w_one, preferred_element_type=jnp.float32)
    act = jax.nn.silu(pre).astype(jnp.bfloat16)
    partial_mix = jnp.dot(act, w_two, preferred_element_type=jnp.float32)
    denoised = (mixed + lax.psum(partial_mix, "neuron")).astype(jnp.bfloat16)
    local_w_two = over_time(act, cotangent)
    dact = jnp.dot(cotangent, w_two.T, preferred_element_type=jnp.float32)
    sig = jax.nn.sigmoid(pre)
    dpre = (dact * sig * (1.0 + pre * (1.0 - sig))).astype(jnp.bfloat16)
    local_w_one = over_time(normed, dpre)
    partial_normed = jnp.dot(dpre, w_one.T, preferred_element_type=jnp.float32)
    dnormed = lax.psum(partial_normed, "neuron")
    local_gain = jnp.sum(dnormed * mixed * scale, axis=0)
    dgained = dnormed * gain[None, :]
    inner = jnp.mean(dgained * mixed, axis=1, keepdims=True)
    dmixed = cotangent.astype(jnp.float32) + scale * dgained - mixed * scale**3 * inner

    def kernel_row(index):
        window = lax.dynamic_slice_in_dim(padded, index, rows, 0)
        return jnp.sum(dmixed * window, axis=0)

    local_kernel = lax.map(kernel_row, jnp.arange(taps, dtype=jnp.int32))
    padded_grad = with_halo(dmixed, (("tm", 0),), half)
    dlifted = (dmixed + conv_time(padded_grad, kernel[::-1], rows)).astype(jnp.bfloat16)
    local_proj = over_time(latent, dlifted)
    dlatent = jnp.dot(dlifted, proj.T, preferred_element_type=jnp.float32).astype(jnp.bfloat16)
    grad_w_one, grad_w_two, grad_gain, grad_kernel, grad_proj = lax.psum(
        (local_w_one, local_w_two, local_gain, local_kernel, local_proj), "tm"
    )
    grad_readin = lax.psum_scatter(
        over_time(signal, dlatent), "tm", scatter_dimension=0, tiled=True
    )
    return (denoised, grad_readin, grad_proj, grad_kernel, grad_gain, grad_w_one, grad_w_two)


def solution(mesh):
    in_specs = (
        P("tm", "neuron"),
        P("neuron", None),
        P(),
        P(),
        P(),
        P(None, "neuron"),
        P("neuron", None),
        P("tm", None),
    )
    out_specs = (
        P("tm", None),
        P(("neuron", "tm"), None),
        P(),
        P(),
        P(),
        P(None, "neuron"),
        P("neuron", None),
    )
    return jax.shard_map(body, mesh=mesh, in_specs=in_specs, out_specs=out_specs, check_vma=False)
```

profile of v0, /device:TPU:1, one launch (start us, length us, event | category | flops | bytes accessed | tf_op | source)
XLA Modules:
  0.0 1194.0 jit_solution(17673050417110770765)
XLA Ops:
  8.8 3.4 fusion.12
  12.2 73.1 %all-reduce.9 = bf16[512,256]{1,0:T(8,128)(2,1)S(1)} all-reduce(f32[512,256]{1,0:T(8,128)S(1)} %fusion.12), channel_id=1, replica_groups=mesh['neuron'=16,'tm'=16] {'neuron'}, use_global_device_ids=true, to_apply=%region_0.0 | all-reduce | flops 131072 | bytes 786432 | tf_op jit(solution)/shard_map/psum | solution.py:42
  86.6 16.6 %collective-permute-start = (f32[31,512]{1,0:T(8,128)S(1)}, f32[31,512]{1,0:T(8,128)S(1)}, u32[]{:S(2)}, u32[]{:S(2)}) collective-permute-start(f32[31,512]{1,0:T(8,128)S(1)} %get-tuple-element.272), channel_id=1, source_target_pairs={{0,1},{1,2},{2,3},{3,4},{4,5},{5,6},{6,7},{7,8},{8,9},{9,10},{10,1... | collective-permute-start | bytes 190472 | tf_op jit(solution)/shard_map/ppermute | solution.py:12
  105.8 3.1 collective-permute-done.1
  110.3 200.2 %while.39 = (s32[]{:T(128)}, f32[512,512]{1,0:T(8,128)}, f32[63,512]{1,0:T(8,128)}, f32[574,512]{1,0:T(8,128)S(1)}, s32[]{:T(128)}, /*index=5*/s32[]{:T(128)}) while((s32[]{:T(128)}, f32[512,512]{1,0:T(8,128)}, f32[63,512]{1,0:T(8,128)}, f32[574,512]{1,0:T(8,128)S(1)}, s32[]{:T(128)}, /*index=5*/s32[]{:T(128)}) %tuple.83), condition=%wide.region_2.0_spmd.clone, body=%wide.region_1.0_spmd.clone.sunk | while | flops 786435 | bytes 3151959 | solution.py:28
  316.9 2.8 rev.3
  322.1 149.1 %all-reduce.8.cloned.1.call-done = (f32[512,512]{1,0:T(8,128)}, f32[512,512]{1,0:T(8,128)}) async-done(((f32[512,512]{1,0:T(8,128)}, f32[512,512]{1,0:T(8,128)}), (f32[512,512]{1,0:T(8,128)}, f32[512,512]{1,0:T(8,128)})) %all-reduce.8.cloned.1.call-update) | async-done | bytes 2097168 | tf_op jit(solution)/shard_map/psum | solution.py:51
  476.0 13.9 %collective-permute-start.2 = (f32[31,512]{1,0:T(8,128)S(1)}, f32[31,512]{1,0:T(8,128)S(1)}, u32[]{:S(2)}, u32[]{:S(2)}) collective-permute-start(f32[31,512]{1,0:T(8,128)S(1)} %get-tuple-element.268), channel_id=1, source_target_pairs={{0,1},{1,2},{2,3},{3,4},{4,5},{5,6},{6,7},{7,8},{8,9},{9,10},{10,1... | collective-permute-start | bytes 190472 | tf_op jit(solution)/shard_map/ppermute | solution.py:12
  496.7 219.1 %while.40 = (s32[]{:T(128)}, f32[512,512]{1,0:T(8,128)}, f32[63,512]{1,0:T(8,128)}, f32[574,512]{1,0:T(8,128)}, s32[]{:T(128)}, /*index=5*/s32[]{:T(128)}) while((s32[]{:T(128)}, f32[512,512]{1,0:T(8,128)}, f32[63,512]{1,0:T(8,128)}, f32[574,512]{1,0:T(8,128)}, s32[]{:T(128)}, /*index=5*/s32[]{:T(128)}) %tuple.86), condition=%wide.region_8.9_spmd.clone, body=%wide.region_7.8_spmd.clone.sunk | while | flops 786435 | bytes 3151959 | solution.py:28
  500.6 2.8 select_add_fusion.5
  504.0 2.8 select_add_fusion.5
  507.5 2.8 select_add_fusion.5
  511.0 2.8 select_add_fusion.5
  514.5 2.8 select_add_fusion.5
  518.0 2.8 select_add_fusion.5
  521.5 2.8 select_add_fusion.5
  524.9 2.8 select_add_fusion.5
  528.4 2.8 select_add_fusion.5
  531.9 2.8 select_add_fusion.5
  535.4 2.8 select_add_fusion.5
  538.9 2.8 select_add_fusion.5
  542.4 2.8 select_add_fusion.5
  545.8 2.8 select_add_fusion.5
  549.3 2.8 select_add_fusion.5
  552.8 2.8 select_add_fusion.5
  556.3 2.8 select_add_fusion.5
  559.8 2.8 select_add_fusion.5
  563.3 2.8 select_add_fusion.5
  566.7 2.8 select_add_fusion.5
  570.2 2.8 select_add_fusion.5
  573.7 2.8 select_add_fusion.5
  577.2 2.8 select_add_fusion.5
  580.7 2.8 select_add_fusion.5
  584.2 2.8 select_add_fusion.5
  587.6 2.8 select_add_fusion.5
  591.1 2.8 select_add_fusion.5
  594.6 2.8 select_add_fusion.5
  598.1 2.8 select_add_fusion.5
  601.6 2.8 select_add_fusion.5
  605.1 2.8 select_add_fusion.5
  608.5 2.8 select_add_fusion.5
  612.0 2.8 select_add_fusion.5
  615.5 2.8 select_add_fusion.5
  619.0 2.8 select_add_fusion.5
  622.5 2.8 select_add_fusion.5
  626.0 2.8 select_add_fusion.5
  629.4 2.8 select_add_fusion.5
  632.9 2.8 select_add_fusion.5
  636.4 2.8 select_add_fusion.5
  639.9 2.8 select_add_fusion.5
  643.4 2.8 select_add_fusion.5
  646.9 2.8 select_add_fusion.5
  650.3 2.8 select_add_fusion.5
  653.8 2.8 select_add_fusion.5
  657.3 2.8 select_add_fusion.5
  660.8 2.8 select_add_fusion.5
  664.3 2.8 select_add_fusion.5
  667.7 2.8 select_add_fusion.5
  671.2 2.8 select_add_fusion.5
  674.7 2.8 select_add_fusion.5
  718.3 6.3 convolution_bitcast_fusion
  724.6 331.9 %while.38 = (s32[]{:T(128)}, f32[63,512]{1,0:T(8,128)}, s32[63]{0:T(128)S(1)}, f32[574,512]{1,0:T(8,128)S(1)}, f32[512,512]{1,0:T(8,128)}, /*index=5*/s32[]{:T(128)}, s32[]{:T(128)}, s32[]{:T(128)}) while((s32[]{:T(128)}, f32[63,512]{1,0:T(8,128)}, s32[63]{0:T(128)S(1)}, f32[574,512]{1,0:T(8,128)S(1)}, f32[512,512]{1,0:T(8,128)}, ...), condition=%wide.region_13.14_spmd, body=%wide.region_11.13_spmd.sunk | while | flops 523781 | bytes 2103435 | solution.py:68
  1058.8 25.6 %psum.61 = f32[512]{0:T(512)} all-reduce(f32[512]{0:T(512)S(1)} %get-tuple-element.232), channel_id=1, replica_groups=mesh['neuron'=16,'tm'=16] {'tm'}, use_global_device_ids=true, to_apply=%region_16.17 | all-reduce | flops 512 | bytes 4096 | tf_op jit(solution)/shard_map/psum | solution.py:73
  1086.2 96.4 %all-reduce.6.cloned.1.call-done = (f32[256,512]{1,0:T(8,128)}, f32[63,512]{1,0:T(8,128)}, f32[512,128]{1,0:T(8,128)}, f32[128,512]{1,0:T(8,128)}) async-done(((f32[256,512]{1,0:T(8,128)}, f32[63,512]{1,0:T(8,128)}, f32[512,128]{1,0:T(8,128)}, f32[128,512]{1,0:T(8,128)}), (f32[256,512]{1,0:T(8,128)}, f32[63,512]{1,0:T(8,128)}, f32[512,128]{1,0:T(8,128)}, f32[128,512]{1,0:T(8,128)})) %all-reduce.6.cloned.1.call-update) | async-done | bytes 1177616 | tf_op jit(solution)/shard_map/psum | solution.py:73
  (465 shorter events, 526.3 us)
Async XLA Ops:
  7.2 1.6 copy-start
  7.2 78.1 %copy-start.6 = (bf16[256,512]{1,0:T(8,128)(2,1)S(1)}, bf16[256,512]{1,0:T(8,128)(2,1)}, u32[]{:S(2)}) copy-start(bf16[256,512]{1,0:T(8,128)(2,1)} %param.16) | copy-start | bytes 786436
  7.2 464.0 %all-reduce.8.cloned.1.call-start = ((), (), s32[]{:S(2)}) async-start(), calls=%async_computation.3 | async-start | bytes 4194304 | tf_op jit(solution)/shard_map/psum | solution.py:51
  85.6 1.0 copy-start.4
  86.6 18.5 %collective-permute-start = (f32[31,512]{1,0:T(8,128)S(1)}, f32[31,512]{1,0:T(8,128)S(1)}, u32[]{:S(2)}, u32[]{:S(2)}) collective-permute-start(f32[31,512]{1,0:T(8,128)S(1)} %get-tuple-element.272), channel_id=1, source_target_pairs={{0,1},{1,2},{2,3},{3,4},{4,5},{5,6},{6,7},{7,8},{8,9},{9,10},{10,1... | collective-permute-start | bytes 190472 | tf_op jit(solution)/shard_map/ppermute | solution.py:12
  103.2 5.7 collective-permute-start.1
  105.2 0.6 copy-start.16
  310.5 1.8 copy-start.11
  310.5 1.8 copy-start.17
  312.2 2.4 copy-start.2
  312.2 1.0 copy-start.15
  312.3 2.3 copy-start.9
  313.3 1.6 copy-start.7
  314.9 0.7 copy-start.12
  316.9 767.5 %reduce-scatter.2.cloned.1.call-start = ((), (), s32[]{:S(2)}) async-start(), calls=%async_computation.1 | async-start | bytes 4456448 | tf_op jit(solution)/shard_map/reduce_scatter | solution.py:76
  471.2 2.1 copy-start.3
  471.2 2.2 copy-start.5
  473.4 18.5 %copy-start.8 = (f32[512,128]{1,0:T(8,128)S(1)}, f32[512,128]{1,0:T(8,128)}, u32[]{:S(2)}) copy-start(f32[512,128]{1,0:T(8,128)} %copy-done.7) | copy-start | bytes 786436
  473.4 18.5 %copy-start.10 = (bf16[512,512]{1,0:T(8,128)(2,1)S(1)}, bf16[512,512]{1,0:T(8,128)(2,1)}, u32[]{:S(2)}) copy-start(bf16[512,512]{1,0:T(8,128)(2,1)} %param.21) | copy-start | bytes 1572868
  476.0 20.6 %copy-start.1 = (f32[512,512]{1,0:T(8,128)}, f32[512,512]{1,0:T(8,128)S(1)}, u32[]{:S(2)}) copy-start(f32[512,512]{1,0:T(8,128)S(1)} %get-tuple-element.397) | copy-start | bytes 3145732
  476.0 16.8 %collective-permute-start.2 = (f32[31,512]{1,0:T(8,128)S(1)}, f32[31,512]{1,0:T(8,128)S(1)}, u32[]{:S(2)}, u32[]{:S(2)}) collective-permute-start(f32[31,512]{1,0:T(8,128)S(1)} %get-tuple-element.268), channel_id=1, source_target_pairs={{0,1},{1,2},{2,3},{3,4},{4,5},{5,6},{6,7},{7,8},{8,9},{9,10},{10,1... | collective-permute-start | bytes 190472 | tf_op jit(solution)/shard_map/ppermute | solution.py:12
  489.9 5.6 collective-permute-start.3
  724.6 458.0 %all-reduce.6.cloned.1.call-start = ((), (), s32[]{:S(2)}) async-start(), calls=%async_computation.2 | async-start | bytes 2359296 | tf_op jit(solution)/shard_map/psum | solution.py:73
  1182.6 3.5 copy-start.14
  1182.6 4.2 copy-start.13
Sparse Core Ops, SparseCore 0:
  317.0 154.1 all-reduce.7
  724.7 68.6 reduce-scatter.1
  1058.9 123.6 all-reduce.5
where the time goes:
time: 1210 us; the launch traced here: 1190 us
  other arithmetic  429 us (35%)
  waiting for transfers between devices  251 us (21%)
  local copies, waits for them, and re-layouts  226 us (19%)
  loops' own time  123 us (10%)
  blocking collectives  98.8 us (8%)
  starting transfers between devices  34.4 us (3%)
  matrix products  18.8 us (2%)
  between operations  14 us (1%)
    add x126, other arithmetic, step(): return total + taps * window  328 us
    psum x1, waiting for transfers between devices, body(): denoised = (mixed + lax.psum(partial_mix, 'neuron')).astype(jnp.bfloat16)  149 us
    another operation x1, loops' own time, body(): local_kernel = lax.map(kernel_row, jnp.arange(taps, dtype=jnp.int32))  123 us
    psum x1, waiting for transfers between devices, body(): lax.psum((local_w_one, local_w_two, local_gain, local_kernel, local_proj)...  96.4 us
    dynamic_slice x126, local copies, waits for them, and re-layouts, step(): taps = lax.dynamic_slice_in_dim(kernel, index, 1, 0)  91 us
    reduce_sum x63, other arithmetic, kernel_row(): return jnp.sum(dmixed * window, axis=0)  88.8 us
    dynamic_update_slice x63, local copies, waits for them, and re-layouts, body(): local_kernel = lax.map(kernel_row, jnp.arange(taps, dtype=jnp.int32))  83.9 us
    psum x1, blocking collectives, body(): latent = lax.psum(partial_latent, 'neuron').astype(jnp.bfloat16)  73.1 us
  transfers between devices with their start and end apart: 7, of which 4 were waited for; matrix products, arithmetic and copies ran while one was open for 18% of the time, Pallas kernels for 0%

commit v1 on v0

--- a/solution.py
+++ b/solution.py
@@ -48,7 +48,7 @@
     pre = jnp.dot(normed, w_one, preferred_element_type=jnp.float32)
     act = jax.nn.silu(pre).astype(jnp.bfloat16)
     partial_mix = jnp.dot(act, w_two, preferred_element_type=jnp.float32)
-    denoised = (mixed + lax.psum(partial_mix, "neuron")).astype(jnp.bfloat16)
+    denoised = (mixed + jnp.sum(lax.all_gather(partial_mix, "neuron"), axis=0)).astype(jnp.bfloat16)
     local_w_two = over_time(act, cotangent)
     dact = jnp.dot(cotangent, w_two.T, preferred_element_type=jnp.float32)
     sig = jax.nn.sigmoid(pre)

time: 1210 us -> 1440 us (1.19)
  waiting for transfers between devices: 251 us -> 470 us
    all_gather x0 -> x1, waiting for transfers between devices: none -> 233 us  [body(): lax.all_gather(partial_mix, 'neuron')]
    ppermute x2, starting transfers between devices: 30.4 us -> 4.72 us  [with_halo(): lax.ppermute(lax.slice_in_dim(block, block.shape[dim] - width, None, axis...]
    ppermute x2, starting transfers between devices: 3.84 us -> 19.3 us  [with_halo(): lax.ppermute(lax.slice_in_dim(block, 0, width, axis=dim), axis, backward)]
  transfers between devices with their start and end apart: 7 -> 8, of which waited for: 4 -> 5; matrix products, arithmetic and copies ran while one was open for 18% -> 16% of each run, Pallas kernels for 0% -> 0%
where the time goes in v1:
time: 1440 us; the launch traced here: 1420 us
  waiting for transfers between devices  470 us (33%)
  other arithmetic  439 us (30%)
  local copies, waits for them, and re-layouts  226 us (16%)
  loops' own time  123 us (9%)
  blocking collectives  101 us (7%)
  starting transfers between devices  24.2 us (2%)
  matrix products  19.6 us (1%)
    add x126, other arithmetic, step(): return total + taps * window  329 us
    all_gather x1, waiting for transfers between devices, body(): lax.all_gather(partial_mix, 'neuron')  233 us
    psum x1, waiting for transfers between devices, body(): dnormed = lax.psum(partial_normed, 'neuron')  141 us
    another operation x1, loops' own time, body(): local_kernel = lax.map(kernel_row, jnp.arange(taps, dtype=jnp.int32))  123 us
    psum x1, waiting for transfers between devices, body(): lax.psum((local_w_one, local_w_two, local_gain, local_kernel, local_proj)...  95.3 us
    dynamic_slice x126, local copies, waits for them, and re-layouts, step(): taps = lax.dynamic_slice_in_dim(kernel, index, 1, 0)  91 us
    reduce_sum x63, other arithmetic, kernel_row(): return jnp.sum(dmixed * window, axis=0)  88.8 us
    dynamic_update_slice x63, local copies, waits for them, and re-layouts, body(): local_kernel = lax.map(kernel_row, jnp.arange(taps, dtype=jnp.int32))  83.9 us
  transfers between devices with their start and end apart: 8, of which 5 were waited for; matrix products, arithmetic and copies ran while one was open for 16% of the time, Pallas kernels for 0%

profile of v1, /device:TPU:1, one launch (start us, length us, event | category | flops | bytes accessed | tf_op | source)
XLA Modules:
  0.0 1417.2 jit_solution(15784245573492275653)
XLA Ops:
  8.8 3.4 fusion.12
  12.2 73.1 %all-reduce.8 = bf16[512,256]{1,0:T(8,128)(2,1)S(1)} all-reduce(f32[512,256]{1,0:T(8,128)S(1)} %fusion.12), channel_id=1, replica_groups=mesh['neuron'=16,'tm'=16] {'neuron'}, use_global_device_ids=true, to_apply=%region_0.0 | all-reduce | flops 131072 | bytes 786432 | tf_op jit(solution)/shard_map/psum | solution.py:42
  86.6 16.0 %collective-permute-start.1 = (f32[31,512]{1,0:T(8,128)S(1)}, f32[31,512]{1,0:T(8,128)S(1)}, u32[]{:S(2)}, u32[]{:S(2)}) collective-permute-start(f32[31,512]{1,0:T(8,128)S(1)} %get-tuple-element.271), channel_id=1, source_target_pairs={{1,0},{2,1},{3,2},{4,3},{5,4},{6,5},{7,6},{8,7},{9,8},{10,9},{11,1... | collective-permute-start | bytes 190472 | tf_op jit(solution)/shard_map/ppermute | solution.py:15
  107.8 199.9 %while.39 = (s32[]{:T(128)}, f32[512,512]{1,0:T(8,128)}, f32[63,512]{1,0:T(8,128)}, f32[574,512]{1,0:T(8,128)S(1)}, s32[]{:T(128)}, /*index=5*/s32[]{:T(128)}) while((s32[]{:T(128)}, f32[512,512]{1,0:T(8,128)}, f32[63,512]{1,0:T(8,128)}, f32[574,512]{1,0:T(8,128)S(1)}, s32[]{:T(128)}, /*index=5*/s32[]{:T(128)}) %tuple.83), condition=%wide.region_2.0_spmd.clone, body=%wide.region_1.0_spmd.clone.sunk | while | flops 786435 | bytes 3151967 | solution.py:28
  320.9 140.9 %all-reduce.5.cloned.1.call-done = f32[512,512]{1,0:T(8,128)} async-done(((f32[512,512]{1,0:T(8,128)}), f32[512,512]{1,0:T(8,128)}) %all-reduce.5.cloned.1.call-update) | async-done | bytes 1048592 | tf_op jit(solution)/shard_map/psum | solution.py:58
  464.3 232.6 %all-gather.3.cloned.1.call-done = f32[8192,512]{1,0:T(8,128)} async-done(((f32[512,512]{1,0:T(8,128)}), f32[8192,512]{1,0:T(8,128)}) %all-gather.3.cloned.1.call-update) | async-done | bytes 16777232 | tf_op jit(solution)/shard_map/all_gather | solution.py:51
  696.9 8.9 reduce_sum.46
  705.8 3.2 multiply_subtract_fusion
  709.0 3.3 collective-permute-start.3
  717.1 220.3 %while.40 = (s32[]{:T(128)}, f32[512,512]{1,0:T(8,128)}, f32[63,512]{1,0:T(8,128)}, f32[574,512]{1,0:T(8,128)}, s32[]{:T(128)}, /*index=5*/s32[]{:T(128)}) while((s32[]{:T(128)}, f32[512,512]{1,0:T(8,128)}, f32[63,512]{1,0:T(8,128)}, f32[574,512]{1,0:T(8,128)}, s32[]{:T(128)}, /*index=5*/s32[]{:T(128)}) %tuple.86), condition=%wide.region_8.9_spmd.clone, body=%wide.region_7.8_spmd.clone.sunk | while | flops 786435 | bytes 3151967 | solution.py:28
  721.0 2.8 select_add_fusion.5
  724.5 2.8 select_add_fusion.5
  728.0 2.8 select_add_fusion.5
  731.5 2.8 select_add_fusion.5
  735.0 2.8 select_add_fusion.5
  738.5 2.8 select_add_fusion.5
  742.0 2.8 select_add_fusion.5
  745.5 2.8 select_add_fusion.5
  749.0 2.8 select_add_fusion.5
  752.5 2.8 select_add_fusion.5
  756.0 2.8 select_add_fusion.5
  759.5 2.8 select_add_fusion.5
  763.0 2.8 select_add_fusion.5
  766.5 2.8 select_add_fusion.5
  770.0 2.8 select_add_fusion.5
  773.5 2.8 select_add_fusion.5
  777.0 2.8 select_add_fusion.5
  780.5 2.8 select_add_fusion.5
  784.0 2.8 select_add_fusion.5
  787.5 2.8 select_add_fusion.5
  791.0 2.8 select_add_fusion.5
  794.5 2.8 select_add_fusion.5
  798.0 2.8 select_add_fusion.5
  801.5 2.8 select_add_fusion.5
  805.0 2.8 select_add_fusion.5
  808.5 2.8 select_add_fusion.5
  812.0 2.8 select_add_fusion.5
  815.5 2.8 select_add_fusion.5
  819.0 2.8 select_add_fusion.5
  822.5 2.8 select_add_fusion.5
  826.0 2.8 select_add_fusion.5
  829.5 2.8 select_add_fusion.5
  833.0 2.8 select_add_fusion.5
  836.6 2.8 select_add_fusion.5
  840.1 2.8 select_add_fusion.5
  843.6 2.8 select_add_fusion.5
  847.1 2.8 select_add_fusion.5
  850.6 2.8 select_add_fusion.5
  854.1 2.8 select_add_fusion.5
  857.6 2.8 select_add_fusion.5
  861.1 2.8 select_add_fusion.5
  864.6 2.8 select_add_fusion.5
  868.1 2.8 select_add_fusion.5
  871.6 2.8 select_add_fusion.5
  885.6 2.8 select_add_fusion.5
  896.1 2.8 select_add_fusion.5
  899.6 2.8 select_add_fusion.5
  910.1 2.8 select_add_fusion.5
  913.6 2.8 select_add_fusion.5
  924.1 2.8 select_add_fusion.5
  939.9 6.2 convolution_bitcast_fusion
  946.2 331.9 %while.38 = (s32[]{:T(128)}, f32[63,512]{1,0:T(8,128)}, s32[63]{0:T(128)S(1)}, f32[574,512]{1,0:T(8,128)S(1)}, f32[512,512]{1,0:T(8,128)}, /*index=5*/s32[]{:T(128)}, s32[]{:T(128)}, s32[]{:T(128)}) while((s32[]{:T(128)}, f32[63,512]{1,0:T(8,128)}, s32[63]{0:T(128)S(1)}, f32[574,512]{1,0:T(8,128)S(1)}, f32[512,512]{1,0:T(8,128)}, ...), condition=%wide.region_13.14_spmd, body=%wide.region_11.13_spmd.sunk | while | flops 523781 | bytes 2103443 | solution.py:68
  1280.3 28.3 %psum.53 = f32[512]{0:T(512)} all-reduce(f32[512]{0:T(512)S(1)} %copy-done.16), channel_id=1, replica_groups=mesh['neuron'=16,'tm'=16] {'tm'}, use_global_device_ids=true, to_apply=%region_16.17 | all-reduce | flops 512 | bytes 4096 | tf_op jit(solution)/shard_map/psum | solution.py:73
  1310.4 95.3 %all-reduce.7.cloned.1.call-done = (f32[256,512]{1,0:T(8,128)}, f32[63,512]{1,0:T(8,128)}, f32[512,128]{1,0:T(8,128)}, f32[128,512]{1,0:T(8,128)}) async-done(((f32[256,512]{1,0:T(8,128)}, f32[63,512]{1,0:T(8,128)}, f32[512,128]{1,0:T(8,128)}, f32[128,512]{1,0:T(8,128)}), (f32[256,512]{1,0:T(8,128)}, f32[63,512]{1,0:T(8,128)}, f32[512,128]{1,0:T(8,128)}, f32[128,512]{1,0:T(8,128)})) %all-reduce.7.cloned.1.call-update) | async-done | bytes 1177616 | tf_op jit(solution)/shard_map/psum | solution.py:73
  (467 shorter events, 530.2 us)
Async XLA Ops:
  7.2 1.6 copy-start
  7.2 78.1 %copy-start.4 = (bf16[256,512]{1,0:T(8,128)(2,1)S(1)}, bf16[256,512]{1,0:T(8,128)(2,1)}, u32[]{:S(2)}) copy-start(bf16[256,512]{1,0:T(8,128)(2,1)} %param.16) | copy-start | bytes 786436
  7.2 454.6 %all-reduce.5.cloned.1.call-start = ((), (), s32[]{:S(2)}) async-start(), calls=%async_computation.1 | async-start | bytes 2097152 | tf_op jit(solution)/shard_map/psum | solution.py:58
  85.6 1.0 copy-start.3
  86.6 18.5 %collective-permute-start.1 = (f32[31,512]{1,0:T(8,128)S(1)}, f32[31,512]{1,0:T(8,128)S(1)}, u32[]{:S(2)}, u32[]{:S(2)}) collective-permute-start(f32[31,512]{1,0:T(8,128)S(1)} %get-tuple-element.271), channel_id=1, source_target_pairs={{1,0},{2,1},{3,2},{4,3},{5,4},{6,5},{7,6},{8,7},{9,8},{10,9},{11,1... | collective-permute-start | bytes 190472 | tf_op jit(solution)/shard_map/ppermute | solution.py:15
  102.7 3.8 collective-permute-start
  105.1 0.6 copy-start.14
  307.8 1.8 copy-start.9
  307.8 1.8 copy-start.15
  309.5 1.8 copy-start.2
  309.6 1.4 copy-start.7
  309.6 1.5 copy-start.13
  310.0 0.7 copy-start.5
  311.4 0.7 copy-start.10
  313.4 383.5 %all-gather.3.cloned.1.call-start = ((), (), s32[]{:S(2)}) async-start(), calls=%async_computation.3 | async-start | bytes 17825792 | tf_op jit(solution)/shard_map/all_gather | solution.py:51
  315.7 992.9 %reduce-scatter.2.cloned.1.call-start = ((), (), s32[]{:S(2)}) async-start(), calls=%async_computation.2 | async-start | bytes 4456448 | tf_op jit(solution)/shard_map/reduce_scatter | solution.py:76
  705.8 8.8 copy-start.6
  705.8 8.8 copy-start.8
  709.0 8.1 copy-start.1
  709.0 6.6 collective-permute-start.3
  712.3 3.6 collective-permute-start.2
  946.1 459.6 %all-reduce.7.cloned.1.call-start = ((), (), s32[]{:S(2)}) async-start(), calls=%async_computation.4 | async-start | bytes 2359296 | tf_op jit(solution)/shard_map/psum | solution.py:73
  1278.1 2.2 copy-start.16
  1405.7 3.5 copy-start.12
  1405.7 4.2 copy-start.11
Sparse Core Ops, SparseCore 0:
  313.5 148.2 all-reduce.4
  464.4 232.4 all-gather.2
  946.2 70.1 reduce-scatter.1
  1280.4 125.2 all-reduce.6
